TPU v7x, 256 devices: a whole 4x4x8 slice. The times are simulated.
256 devices in a mesh: gx: 16 (over x, z_hi, core), gy: 4 (over z_lo), gz: 4 (over y).
Axes of the slice: x: 4, y: 4, z: 8 (z_hi: 2, z_lo: 4; z = z_hi * 4 + z_lo), core: 2. Of those that a mesh axis runs over, the one named last changes fastest.
Arguments:
- image_slab: float32 [64, 1024, 1024], P(('gz', 'gx'), None, 'gy'), may hold values from -6 to 6
- deformed_slab: float32 [64, 1024, 1024], P(('gz', 'gx'), None, 'gy'), may hold values from -6 to 6
- shifts: int32 [2, 3, 4, 16, 4], P(None, None, 'gz', 'gx', 'gy'), may hold values from -8 to 8, as said below
Outputs:
- displacement: float32 [3, 12, 144, 132], P(None, 'gz', 'gx', 'gy')
- residual_map: float32 [64, 1024, 1024], P('gz', 'gx', 'gy')
Inputs may be any that keep to these rules, and one draw needn't show every extreme that they name: `shifts`: every component lies within -8 to 8, and both ends are taken by some entry.
All inputs are finite; a program needn't handle non-finite values.
Results may differ from a plain program's by a relative error of at most 0.0003.
Values sent between devices are 32-bit elements; how exact they have to be, the bound alone decides.
No kernel may reach another device: no remote copies, remote signals or barrier semaphores. Data moves between devices by JAX's collectives and lax.ppermute only.
A program may use at most 128 MiB of HBM per device.

v0:
```python
import jax
import jax.numpy as jnp
from jax import lax
from jax.sharding import PartitionSpec as P

ELEMENT = 8
DMAX = 8
ITERS = 2
SWEEPS = 3
DAMPING = 0.7
REGULARIZE = 4.0


def padded(block, sides, width):
    for axis, dim in sides:
        count = lax.axis_size(axis)
        forward = [(i, i + 1) for i in range(count - 1)]
        backward = [(target, source) for source, target in forward]
        low = lax.ppermute(
            lax.slice_in_dim(block, block.shape[dim] - width, None, axis=dim), axis, forward
        )
        high = lax.ppermute(lax.slice_in_dim(block, 0, width, axis=dim), axis, backward)
        block = jnp.concatenate([low, block, high], axis=dim)
    return block


def node_weights(squared):
    fraction = (jnp.arange(ELEMENT, dtype=jnp.float32) + 0.5) / ELEMENT
    lower_weight = 1.0 - fraction
    if squared:
        return (lower_weight * lower_weight, fraction * fraction)
    return (lower_weight, fraction)


def weight_shape(weight, ndim, axis):
    shape = [1] * (ndim + 1)
    shape[axis + 1] = ELEMENT
    return weight.reshape(shape)


def spread_axis(nodal, axis, weights):
    count = nodal.shape[axis] - 1
    lower = jnp.expand_dims(lax.slice_in_dim(nodal, 0, count, axis=axis), axis + 1)
    upper = jnp.expand_dims(lax.slice_in_dim(nodal, 1, count + 1, axis=axis), axis + 1)
    ndim = nodal.ndim
    joined = lower * weight_shape(weights[0], ndim, axis) + upper * weight_shape(
        weights[1], ndim, axis
    )
    shape = list(nodal.shape)
    shape[axis] = count * ELEMENT
    return joined.reshape(shape)


def collect_axis(field, axis, weights):
    count = field.shape[axis] // ELEMENT
    shape = list(field.shape)
    split_shape = shape[:axis] + [count, ELEMENT] + shape[axis + 1 :]
    blocks = field.reshape(split_shape)
    ndim = field.ndim
    lower = jnp.sum(blocks * weight_shape(weights[0], ndim, axis), axis=axis + 1)
    upper = jnp.sum(blocks * weight_shape(weights[1], ndim, axis), axis=axis + 1)
    pad_low = [(0, 0)] * ndim
    pad_high = [(0, 0)] * ndim
    pad_low[axis] = (0, 1)
    pad_high[axis] = (1, 0)
    return jnp.pad(lower, pad_low) + jnp.pad(upper, pad_high)


def cut_range(array, axis, start, length):
    return lax.slice_in_dim(array, start, start + length, axis=axis)


def smooth(array, axis):
    length = array.shape[axis] - 2
    return (
        cut_range(array, axis, 0, length)
        + 2.0 * cut_range(array, axis, 1, length)
        + cut_range(array, axis, 2, length)
    ) * 0.25


def differ(array, axis):
    length = array.shape[axis] - 2
    return (cut_range(array, axis, 2, length) - cut_range(array, axis, 0, length)) * 0.5


def gradients(extended):
    along_z = smooth(smooth(differ(extended, 0), 1), 2)
    along_x = smooth(smooth(differ(extended, 1), 0), 2)
    along_y = smooth(smooth(differ(extended, 2), 0), 1)
    return jnp.stack([along_z, along_x, along_y])


def interpolate(nodal, weights):
    step = spread_axis(nodal, 3, weights)
    step = spread_axis(step, 2, weights)
    return spread_axis(step, 1, weights)


def restrict(field, weights):
    step = collect_axis(field, 1, weights)
    step = collect_axis(step, 2, weights)
    return collect_axis(step, 3, weights)


def fold_rims(extended, axis):
    moved = jnp.moveaxis(extended, axis, 0)
    inner = moved[1:-1]
    inner = inner.at[0].add(moved[0])
    inner = inner.at[-1].add(moved[-1])
    return jnp.moveaxis(inner, 0, axis)


def share(partial_value):
    extended = padded(partial_value, (("gx", 2), ("gy", 3), ("gz", 1)), 1)
    for axis in (1, 2, 3):
        extended = fold_rims(extended, axis)
    return extended


def invert(diag):
    a, b, c, d, e, f = (diag[0], diag[1], diag[2], diag[3], diag[4], diag[5])
    i00 = b * c - f * f
    i11 = a * c - e * e
    i22 = a * b - d * d
    i01 = e * f - d * c
    i02 = d * f - b * e
    i12 = d * e - a * f
    det = a * i00 + d * i01 + e * i02
    return jnp.stack([i00, i11, i22, i01, i02, i12]) / det


def apply_inverse(inverse, vector):
    out_z = inverse[0] * vector[0] + inverse[3] * vector[1] + inverse[4] * vector[2]
    out_x = inverse[3] * vector[0] + inverse[1] * vector[1] + inverse[5] * vector[2]
    out_y = inverse[4] * vector[0] + inverse[5] * vector[1] + inverse[2] * vector[2]
    return jnp.stack([out_z, out_x, out_y])


def shards(image_slab, deformed_slab, shifts):
    image, deformed_block = (
        lax.all_to_all(image_slab, "gx", split_axis=1, concat_axis=0, tiled=True),
        lax.all_to_all(deformed_slab, "gx", split_axis=1, concat_axis=0, tiled=True),
    )
    z_count, x_count, y_count = image.shape
    image_ext = padded(image, (("gx", 1), ("gy", 2), ("gz", 0)), 1)
    deformed_ext = padded(deformed_block, (("gx", 1), ("gy", 2), ("gz", 0)), DMAX)
    grads = gradients(image_ext)
    weights = node_weights(False)
    squared = node_weights(True)
    pairs = ((0, 0), (1, 1), (2, 2), (0, 1), (0, 2), (1, 2))
    products = jnp.stack([grads[i] * grads[j] for i, j in pairs])
    diag = share(restrict(products, squared))
    diag = (
        diag
        + REGULARIZE * jnp.array([1.0, 1.0, 1.0, 0.0, 0.0, 0.0], jnp.float32)[:, None, None, None]
    )
    inverse = invert(diag)
    nodal = jnp.zeros(
        (3, z_count // ELEMENT + 1, x_count // ELEMENT + 1, y_count // ELEMENT + 1), jnp.float32
    )

    def residual(nodal_now, warped_now, offset):
        moved = interpolate(nodal_now, weights)
        offset_float = offset.astype(jnp.float32)[:, None, None, None]
        return image - warped_now - jnp.sum(grads * (moved - offset_float), axis=0)

    warped = image
    offset = shifts[0, :, 0, 0, 0]
    for iteration in range(ITERS):
        offset = shifts[iteration, :, 0, 0, 0]
        starts = [DMAX + offset[0], DMAX + offset[1], DMAX + offset[2]]
        warped = lax.dynamic_slice(deformed_ext, starts, (z_count, x_count, y_count))
        resid = residual(nodal, warped, offset)
        rhs = share(restrict(grads * resid[None], weights))
        delta = DAMPING * apply_inverse(inverse, rhs)
        for sweep in range(SWEEPS - 1):
            inner = jnp.sum(grads * interpolate(delta, weights), axis=0)
            applied = share(restrict(grads * inner[None], weights)) + REGULARIZE * delta
            delta = delta + DAMPING * apply_inverse(inverse, rhs - applied)
        nodal = nodal + delta
    final = residual(nodal, warped, offset)
    return (nodal, final)


def solution(mesh):
    return jax.shard_map(
        shards,
        mesh=mesh,
        in_specs=(
            P(("gz", "gx"), None, "gy"),
            P(("gz", "gx"), None, "gy"),
            P(None, None, "gz", "gx", "gy"),
        ),
        out_specs=(P(None, "gz", "gx", "gy"), P("gz", "gx", "gy")),
        check_vma=False,
    )
```

profile of v0, /device:TPU:1, one launch (start us, length us, event | category | flops | bytes accessed | tf_op | source)
XLA Modules:
  0.0 511.1 jit_solution(6681661447291161037)
XLA Ops:
  0.6 3.4 copy.154
  4.0 12.4 %all-to-all-start = ((f32[1,1024,256]{2,0,1:T(1,128)}), f32[1,1024,256]{2,0,1:T(1,128)S(1)}, u32[]{:S(2)}, u32[]{:S(2)}) async-start(f32[1,1024,256]{2,0,1:T(1,128)} %copy.154), calls=%async_computation | async-start | bytes 2097152 | tf_op jit(solution)/shard_map/all_to_all | solution.py:142
  18.5 19.8 %all-to-all-done = f32[1,1024,256]{2,0,1:T(1,128)S(1)} async-done(((f32[1,1024,256]{2,0,1:T(1,128)}), f32[1,1024,256]{2,0,1:T(1,128)S(1)}, u32[]{:S(2)}, u32[]{:S(2)}) %all-to-all-start) | async-done | bytes 1048608 | tf_op jit(solution)/shard_map/all_to_all | solution.py:142
  38.2 5.1 all-to-all-start.1
  45.2 7.5 %collective-permute-start = (f32[16,1,256]{2,1,0:T(1,128)S(1)}, f32[16,1,256]{2,1,0:T(1,128)S(1)}, u32[]{:S(2)}, u32[]{:S(2)}) collective-permute-start(f32[16,1,256]{2,1,0:T(1,128)S(1)} %get-tuple-element.579), channel_id=1, source_target_pairs={{0,16},{16,32},{32,48},{48,64},{64,80},{80,96},{96,112},{112,128},... | collective-permute-start | bytes 49160 | tf_op jit(solution)/shard_map/ppermute | solution.py:19
  55.3 11.6 %collective-permute-done.1 = f32[16,1,256]{2,1,0:T(1,128)S(1)} collective-permute-done((f32[16,1,256]{2,1,0:T(1,128)S(1)}, f32[16,1,256]{2,1,0:T(1,128)S(1)}, u32[]{:S(2)}, u32[]{:S(2)}) %collective-permute-start.1) | collective-permute-done | bytes 16416 | tf_op jit(solution)/shard_map/ppermute | solution.py:22
  69.3 10.0 %collective-permute-start.2 = (f32[16,66,1]{1,0,2:T(8,128)S(1)}, f32[16,66,1]{1,0,2:T(8,128)S(1)}, u32[]{:S(2)}, u32[]{:S(2)}) collective-permute-start(f32[16,66,1]{1,0,2:T(8,128)S(1)} %copy.155), channel_id=1, source_target_pairs={{0,4},{4,8},{8,12},{1,5},{5,9},{9,13},{2,6},{6,10},{10,14},{3,7},{... | collective-permute-start | bytes 12680 | tf_op jit(solution)/shard_map/ppermute | solution.py:19
  88.7 4.9 collective-permute-start.5
  100.8 2.3 fusion.2
  108.2 3.5 reshape.1873
  111.8 3.3 multiply_reduce_fusion.21
  115.2 3.6 collective-permute-start.6
  120.8 6.9 %collective-permute-done.7 = f32[6,3,1,33]{3,0,2,1:T(8,128)S(1)} collective-permute-done((f32[6,3,1,33]{3,0,2,1:T(8,128)S(1)}, f32[6,3,1,33]{3,0,2,1:T(8,128)S(1)}, u32[]{:S(2)}, u32[]{:S(2)}) %collective-permute-start.7) | collective-permute-done | bytes 2408 | tf_op jit(solution)/shard_map/ppermute | solution.py:22
  127.8 4.4 collective-permute-start.8
  138.0 2.6 collective-permute-start.10
  143.6 2.5 collective-permute-done.11
  150.0 6.3 %collective-permute-start.14 = (f32[16,80,8]{1,2,0:T(8,128)S(1)}, f32[16,80,8]{1,2,0:T(8,128)S(1)}, u32[]{:S(2)}, u32[]{:S(2)}) collective-permute-start(f32[16,80,8]{1,2,0:T(8,128)S(1)} %copy.163), channel_id=1, source_target_pairs={{0,4},{4,8},{8,12},{1,5},{5,9},{9,13},{2,6},{6,10},{10,14},{3,7},{... | collective-permute-start | bytes 122888 | tf_op jit(solution)/shard_map/ppermute | solution.py:19
  160.6 2.9 collective-permute-done.15
  165.4 2.4 pad_maximum_fusion.3
  169.3 3.6 collective-permute-start.16
  179.1 3.5 scatter-add.149
  185.0 8.9 %collective-permute-done.16 = f32[8,80,272]{2,1,0:T(8,128)} collective-permute-done((f32[8,80,272]{2,1,0:T(8,128)}, f32[8,80,272]{2,1,0:T(8,128)}, u32[]{:S(2)}, u32[]{:S(2)}) %collective-permute-start.16) | collective-permute-done | bytes 696352 | tf_op jit(solution)/shard_map/ppermute | solution.py:19
  193.8 4.8 collective-permute-done.17
  198.6 3.6 pad_maximum_fusion
  208.8 8.4 %collective-permute-start.18 = (f32[3,3,1,33]{3,0,2,1:T(4,128)S(1)}, f32[3,3,1,33]{3,0,2,1:T(4,128)S(1)}, u32[]{:S(2)}, u32[]{:S(2)}) collective-permute-start(f32[3,3,1,33]{3,0,2,1:T(4,128)S(1)} %get-tuple-element.656), channel_id=1, source_target_pairs={{0,16},{16,32},{32,48},{48,64},{64,80},{80,96},{96,112},{112,128},... | collective-permute-start | bytes 3572 | tf_op jit(solution)/shard_map/ppermute | solution.py:19
  219.2 6.8 %collective-permute-done.19 = f32[3,3,1,33]{3,0,2,1:T(4,128)S(1)} collective-permute-done((f32[3,3,1,33]{3,0,2,1:T(4,128)S(1)}, f32[3,3,1,33]{3,0,2,1:T(4,128)S(1)}, u32[]{:S(2)}, u32[]{:S(2)}) %collective-permute-start.19) | collective-permute-done | bytes 1220 | tf_op jit(solution)/shard_map/ppermute | solution.py:22
  230.8 3.5 collective-permute-done.21
  238.1 3.2 collective-permute-done.23
  243.0 2.6 scatter-add.159
  252.3 2.7 mul.1701
  262.1 4.4 collective-permute-start.24
  268.6 6.8 %collective-permute-done.25 = f32[3,3,1,33]{3,0,2,1:T(4,128)S(1)} collective-permute-done((f32[3,3,1,33]{3,0,2,1:T(4,128)S(1)}, f32[3,3,1,33]{3,0,2,1:T(4,128)S(1)}, u32[]{:S(2)}, u32[]{:S(2)}) %collective-permute-start.25) | collective-permute-done | bytes 1220 | tf_op jit(solution)/shard_map/ppermute | solution.py:22
  275.6 3.5 collective-permute-start.26
  280.4 3.7 collective-permute-done.27
  284.3 3.0 collective-permute-start.28
  288.6 3.2 collective-permute-done.29
  301.8 2.7 mul.1741
  311.6 5.5 %collective-permute-start.30 = (f32[3,3,1,33]{3,0,2,1:T(4,128)S(1)}, f32[3,3,1,33]{3,0,2,1:T(4,128)S(1)}, u32[]{:S(2)}, u32[]{:S(2)}) collective-permute-start(f32[3,3,1,33]{3,0,2,1:T(4,128)S(1)} %get-tuple-element.645), channel_id=1, source_target_pairs={{0,16},{16,32},{32,48},{48,64},{64,80},{80,96},{96,112},{112,128},... | collective-permute-start | bytes 3572 | tf_op jit(solution)/shard_map/ppermute | solution.py:19
  319.2 6.8 %collective-permute-done.31 = f32[3,3,1,33]{3,0,2,1:T(4,128)S(1)} collective-permute-done((f32[3,3,1,33]{3,0,2,1:T(4,128)S(1)}, f32[3,3,1,33]{3,0,2,1:T(4,128)S(1)}, u32[]{:S(2)}, u32[]{:S(2)}) %collective-permute-start.31) | collective-permute-done | bytes 1220 | tf_op jit(solution)/shard_map/ppermute | solution.py:22
  328.9 3.7 collective-permute-done.33
  363.3 5.2 %collective-permute-start.36 = (f32[3,3,1,33]{3,0,2,1:T(4,128)S(1)}, f32[3,3,1,33]{3,0,2,1:T(4,128)S(1)}, u32[]{:S(2)}, u32[]{:S(2)}) collective-permute-start(f32[3,3,1,33]{3,0,2,1:T(4,128)S(1)} %get-tuple-element.641), channel_id=1, source_target_pairs={{0,16},{16,32},{32,48},{48,64},{64,80},{80,96},{96,112},{112,128},... | collective-permute-start | bytes 3572 | tf_op jit(solution)/shard_map/ppermute | solution.py:19
  370.6 6.8 %collective-permute-done.37 = f32[3,3,1,33]{3,0,2,1:T(4,128)S(1)} collective-permute-done((f32[3,3,1,33]{3,0,2,1:T(4,128)S(1)}, f32[3,3,1,33]{3,0,2,1:T(4,128)S(1)}, u32[]{:S(2)}, u32[]{:S(2)}) %collective-permute-start.37) | collective-permute-done | bytes 1220 | tf_op jit(solution)/shard_map/ppermute | solution.py:22
  380.2 3.7 collective-permute-done.39
  384.0 3.2 collective-permute-start.40
  388.5 3.2 collective-permute-done.41
  392.6 2.3 scatter-add.189
  396.7 2.7 mul.1810
  400.9 2.7 mul.1813
  407.3 2.7 reshape.1883
  412.3 4.8 collective-permute-start.42
  419.1 6.8 %collective-permute-done.43 = f32[3,3,1,33]{3,0,2,1:T(4,128)S(1)} collective-permute-done((f32[3,3,1,33]{3,0,2,1:T(4,128)S(1)}, f32[3,3,1,33]{3,0,2,1:T(4,128)S(1)}, u32[]{:S(2)}, u32[]{:S(2)}) %collective-permute-start.43) | collective-permute-done | bytes 1220 | tf_op jit(solution)/shard_map/ppermute | solution.py:22
  429.3 3.7 collective-permute-done.45
  435.8 3.2 collective-permute-done.47
  441.9 3.3 scatter-add.199
  447.7 2.7 mul.1846
  452.0 2.7 mul.1849
  458.4 2.7 reshape.1885
  463.4 4.8 collective-permute-start.48
  470.2 6.8 %collective-permute-done.49 = f32[3,3,1,33]{3,0,2,1:T(4,128)S(1)} collective-permute-done((f32[3,3,1,33]{3,0,2,1:T(4,128)S(1)}, f32[3,3,1,33]{3,0,2,1:T(4,128)S(1)}, u32[]{:S(2)}, u32[]{:S(2)}) %collective-permute-start.49) | collective-permute-done | bytes 1220 | tf_op jit(solution)/shard_map/ppermute | solution.py:22
  480.1 3.7 collective-permute-done.51
  483.9 2.5 collective-permute-start.52
  487.7 3.2 collective-permute-done.53
  493.8 2.8 scatter-add.209
  508.1 2.8 bitcast_subtract_fusion
  (484 shorter events, 201.2 us)
Async XLA Ops:
  4.0 34.2 %all-to-all-start = ((f32[1,1024,256]{2,0,1:T(1,128)}), f32[1,1024,256]{2,0,1:T(1,128)S(1)}, u32[]{:S(2)}, u32[]{:S(2)}) async-start(f32[1,1024,256]{2,0,1:T(1,128)} %copy.154), calls=%async_computation | async-start | bytes 2097152 | tf_op jit(solution)/shard_map/all_to_all | solution.py:142
  18.5 36.1 %copy-start.44 = (s32[2,3,1,1,1]{1,4,3,2,0:T(1,128)S(1)}, s32[2,3,1,1,1]{1,4,3,2,0:T(1,128)}, u32[]{:S(2)}) copy-start(s32[2,3,1,1,1]{1,4,3,2,0:T(1,128)} %param.90) | copy-start | bytes 76
  38.2 55.3 %all-to-all-start.1 = ((f32[1,1024,256]{2,0,1:T(1,128)}), f32[1,1024,256]{2,0,1:T(1,128)}, u32[]{:S(2)}, u32[]{:S(2)}) async-start(f32[1,1024,256]{2,0,1:T(1,128)} %copy.162), calls=%async_computation.1 | async-start | bytes 2097152 | tf_op jit(solution)/shard_map/all_to_all | solution.py:143
  45.1 54.6 %copy-start = (f32[1,1024,256]{2,1,0:T(8,128)}, f32[1,1024,256]{2,1,0:T(8,128)S(1)}, u32[]{:S(2)}) copy-start(f32[1,1024,256]{2,1,0:T(8,128)S(1)} %copy.210) | copy-start | bytes 3145732
  45.2 10.1 %collective-permute-start = (f32[16,1,256]{2,1,0:T(1,128)S(1)}, f32[16,1,256]{2,1,0:T(1,128)S(1)}, u32[]{:S(2)}, u32[]{:S(2)}) collective-permute-start(f32[16,1,256]{2,1,0:T(1,128)S(1)} %get-tuple-element.579), channel_id=1, source_target_pairs={{0,16},{16,32},{32,48},{48,64},{64,80},{80,96},{96,112},{112,128},... | collective-permute-start | bytes 49160 | tf_op jit(solution)/shard_map/ppermute | solution.py:19
  52.6 14.2 %collective-permute-start.1 = (f32[16,1,256]{2,1,0:T(1,128)S(1)}, f32[16,1,256]{2,1,0:T(1,128)S(1)}, u32[]{:S(2)}, u32[]{:S(2)}) collective-permute-start(f32[16,1,256]{2,1,0:T(1,128)S(1)} %get-tuple-element.580), channel_id=1, source_target_pairs={{16,0},{32,16},{48,32},{64,48},{80,64},{96,80},{112,96},{128,112},... | collective-permute-start | bytes 49160 | tf_op jit(solution)/shard_map/ppermute | solution.py:22
  69.3 17.2 %collective-permute-start.2 = (f32[16,66,1]{1,0,2:T(8,128)S(1)}, f32[16,66,1]{1,0,2:T(8,128)S(1)}, u32[]{:S(2)}, u32[]{:S(2)}) collective-permute-start(f32[16,66,1]{1,0,2:T(8,128)S(1)} %copy.155), channel_id=1, source_target_pairs={{0,4},{4,8},{8,12},{1,5},{5,9},{9,13},{2,6},{6,10},{10,14},{3,7},{... | collective-permute-start | bytes 12680 | tf_op jit(solution)/shard_map/ppermute | solution.py:19
  79.6 7.3 %collective-permute-start.3 = (f32[16,66,1]{1,0,2:T(8,128)S(1)}, f32[16,66,1]{1,0,2:T(8,128)S(1)}, u32[]{:S(2)}, u32[]{:S(2)}) collective-permute-start(f32[16,66,1]{1,0,2:T(8,128)S(1)} %copy.156), channel_id=1, source_target_pairs={{4,0},{8,4},{12,8},{5,1},{9,5},{13,9},{6,2},{10,6},{14,10},{7,3},{... | collective-permute-start | bytes 12680 | tf_op jit(solution)/shard_map/ppermute | solution.py:22
  87.4 8.5 %collective-permute-start.4 = (f32[1,66,258]{2,1,0:T(8,128)S(1)}, f32[1,66,258]{2,1,0:T(8,128)S(1)}, u32[]{:S(2)}, u32[]{:S(2)}) collective-permute-start(f32[1,66,258]{2,1,0:T(8,128)S(1)} %get-tuple-element.566), channel_id=1, source_target_pairs={{1,0},{2,1},{3,2},{5,4},{6,5},{7,6},{9,8},{10,9},{11,10},{13,12},{... | collective-permute-start | bytes 204344 | tf_op jit(solution)/shard_map/ppermute | solution.py:22
  88.7 7.8 %collective-permute-start.5 = (f32[1,66,258]{2,1,0:T(8,128)S(1)}, f32[1,66,258]{2,1,0:T(8,128)}, u32[]{:S(2)}, u32[]{:S(2)}) collective-permute-start(f32[1,66,258]{2,1,0:T(8,128)S(1)} %get-tuple-element.565), channel_id=1, source_target_pairs={{0,1},{1,2},{2,3},{4,5},{5,6},{6,7},{8,9},{9,10},{10,11},{12,13},{... | collective-permute-start | bytes 204344 | tf_op jit(solution)/shard_map/ppermute | solution.py:19
  111.8 30.1 %copy-start.11 = (f32[3,2,64,256]{3,2,1,0:T(8,128)S(1)}, f32[3,2,64,256]{3,2,1,0:T(8,128)}, u32[]{:S(2)}) copy-start(f32[3,2,64,256]{3,2,1,0:T(8,128)} %get-tuple-element.594) | copy-start | bytes 1179652
  111.8 30.2 %copy-start.46 = (f32[3]{0:T(128)S(1)}, f32[3]{0:T(128)}, u32[]{:S(2)}) copy-start(f32[3]{0:T(128)} %get-tuple-element.689) | copy-start | bytes 40
  115.2 5.6 %collective-permute-start.6 = (f32[6,3,1,33]{3,0,2,1:T(8,128)S(1)}, f32[6,3,1,33]{3,0,2,1:T(8,128)S(1)}, u32[]{:S(2)}, u32[]{:S(2)}) collective-permute-start(f32[6,3,1,33]{3,0,2,1:T(8,128)S(1)} %get-tuple-element.597), channel_id=1, source_target_pairs={{0,16},{16,32},{32,48},{48,64},{64,80},{80,96},{96,112},{112,128},... | collective-permute-start | bytes 7136 | tf_op jit(solution)/shard_map/ppermute | solution.py:19
  118.7 8.9 %collective-permute-start.7 = (f32[6,3,1,33]{3,0,2,1:T(8,128)S(1)}, f32[6,3,1,33]{3,0,2,1:T(8,128)S(1)}, u32[]{:S(2)}, u32[]{:S(2)}) collective-permute-start(f32[6,3,1,33]{3,0,2,1:T(8,128)S(1)} %get-tuple-element.598), channel_id=1, source_target_pairs={{16,0},{32,16},{48,32},{64,48},{80,64},{96,80},{112,96},{128,112},... | collective-permute-start | bytes 7136 | tf_op jit(solution)/shard_map/ppermute | solution.py:22
  127.8 10.1 %collective-permute-start.8 = (f32[6,3,11,1]{3,0,2,1:T(8,128)S(1)}, f32[6,3,11,1]{3,0,2,1:T(8,128)S(1)}, u32[]{:S(2)}, u32[]{:S(2)}) collective-permute-start(f32[6,3,11,1]{3,0,2,1:T(8,128)S(1)} %get-tuple-element.629), channel_id=1, source_target_pairs={{0,4},{4,8},{8,12},{1,5},{5,9},{9,13},{2,6},{6,10},{10,14},{3,7},{... | collective-permute-start | bytes 2384 | tf_op jit(solution)/shard_map/ppermute | solution.py:19
  132.1 5.8 %collective-permute-start.9 = (f32[6,3,11,1]{3,0,2,1:T(8,128)S(1)}, f32[6,3,11,1]{3,0,2,1:T(8,128)S(1)}, u32[]{:S(2)}, u32[]{:S(2)}) collective-permute-start(f32[6,3,11,1]{3,0,2,1:T(8,128)S(1)} %get-tuple-element.630), channel_id=1, source_target_pairs={{4,0},{8,4},{12,8},{5,1},{9,5},{13,9},{6,2},{10,6},{14,10},{7,3},{... | collective-permute-start | bytes 2384 | tf_op jit(solution)/shard_map/ppermute | solution.py:22
  133.5 12.8 %collective-permute-start.12 = (f32[16,8,256]{2,1,0:T(8,128)S(1)}, f32[16,8,256]{2,1,0:T(8,128)S(1)}, u32[]{:S(2)}, u32[]{:S(2)}) collective-permute-start(f32[16,8,256]{2,1,0:T(8,128)S(1)} %get-tuple-element.577), channel_id=1, source_target_pairs={{0,16},{16,32},{32,48},{48,64},{64,80},{80,96},{96,112},{112,128},... | collective-permute-start | bytes 393224 | tf_op jit(solution)/shard_map/ppermute | solution.py:19
  135.6 11.7 %collective-permute-start.13 = (f32[16,8,256]{2,1,0:T(8,128)S(1)}, f32[16,8,256]{2,1,0:T(8,128)S(1)}, u32[]{:S(2)}, u32[]{:S(2)}) collective-permute-start(f32[16,8,256]{2,1,0:T(8,128)S(1)} %get-tuple-element.578), channel_id=1, source_target_pairs={{16,0},{32,16},{48,32},{64,48},{80,64},{96,80},{112,96},{128,112},... | collective-permute-start | bytes 393224 | tf_op jit(solution)/shard_map/ppermute | solution.py:22
  138.0 5.6 %collective-permute-start.10 = (f32[6,1,11,35]{3,0,2,1:T(8,128)S(1)}, f32[6,1,11,35]{3,0,2,1:T(8,128)S(1)}, u32[]{:S(2)}, u32[]{:S(2)}) collective-permute-start(f32[6,1,11,35]{3,0,2,1:T(8,128)S(1)} %get-tuple-element.595), channel_id=1, source_target_pairs={{0,1},{1,2},{2,3},{4,5},{5,6},{6,7},{8,9},{9,10},{10,11},{12,13},{... | collective-permute-start | bytes 27728 | tf_op jit(solution)/shard_map/ppermute | solution.py:19
  140.6 5.5 %collective-permute-start.11 = (f32[6,1,11,35]{3,0,2,1:T(8,128)S(1)}, f32[6,1,11,35]{3,0,2,1:T(8,128)S(1)}, u32[]{:S(2)}, u32[]{:S(2)}) collective-permute-start(f32[6,1,11,35]{3,0,2,1:T(8,128)S(1)} %get-tuple-element.596), channel_id=1, source_target_pairs={{1,0},{2,1},{3,2},{5,4},{6,5},{7,6},{9,8},{10,9},{11,10},{13,12},{... | collective-permute-start | bytes 27728 | tf_op jit(solution)/shard_map/ppermute | solution.py:22
  150.0 9.5 %collective-permute-start.14 = (f32[16,80,8]{1,2,0:T(8,128)S(1)}, f32[16,80,8]{1,2,0:T(8,128)S(1)}, u32[]{:S(2)}, u32[]{:S(2)}) collective-permute-start(f32[16,80,8]{1,2,0:T(8,128)S(1)} %copy.163), channel_id=1, source_target_pairs={{0,4},{4,8},{8,12},{1,5},{5,9},{9,13},{2,6},{6,10},{10,14},{3,7},{... | collective-permute-start | bytes 122888 | tf_op jit(solution)/shard_map/ppermute | solution.py:19
  158.2 5.3 %collective-permute-start.15 = (f32[16,80,8]{1,2,0:T(8,128)}, f32[16,80,8]{1,2,0:T(8,128)}, u32[]{:S(2)}, u32[]{:S(2)}) collective-permute-start(f32[16,80,8]{1,2,0:T(8,128)} %copy.164), channel_id=1, source_target_pairs={{4,0},{8,4},{12,8},{5,1},{9,5},{13,9},{6,2},{10,6},{14,10},{7,3},{... | collective-permute-start | bytes 122888 | tf_op jit(solution)/shard_map/ppermute | solution.py:22
  167.9 30.8 %copy-start.13 = (f32[16,8,256]{2,1,0:T(8,128)S(1)}, f32[16,8,256]{2,1,0:T(8,128)}, u32[]{:S(2)}) copy-start(f32[16,8,256]{2,1,0:T(8,128)} %copy-done.12) | copy-start | bytes 393220
  167.9 30.8 %copy-start.15 = (f32[16,8,256]{2,1,0:T(8,128)S(1)}, f32[16,8,256]{2,1,0:T(8,128)}, u32[]{:S(2)}) copy-start(f32[16,8,256]{2,1,0:T(8,128)} %copy-done.14) | copy-start | bytes 393220
  169.3 24.5 %collective-permute-start.16 = (f32[8,80,272]{2,1,0:T(8,128)}, f32[8,80,272]{2,1,0:T(8,128)}, u32[]{:S(2)}, u32[]{:S(2)}) collective-permute-start(f32[8,80,272]{2,1,0:T(8,128)} %get-tuple-element.570), channel_id=1, source_target_pairs={{0,1},{1,2},{2,3},{4,5},{5,6},{6,7},{8,9},{9,10},{10,11},{12,13},{... | collective-permute-start | bytes 2088968 | tf_op jit(solution)/shard_map/ppermute | solution.py:19
  172.9 25.7 %collective-permute-start.17 = (f32[8,80,272]{2,1,0:T(8,128)}, f32[8,80,272]{2,1,0:T(8,128)}, u32[]{:S(2)}, u32[]{:S(2)}) collective-permute-start(f32[8,80,272]{2,1,0:T(8,128)} %get-tuple-element.571), channel_id=1, source_target_pairs={{1,0},{2,1},{3,2},{5,4},{6,5},{7,6},{9,8},{10,9},{11,10},{13,12},{... | collective-permute-start | bytes 2088968 | tf_op jit(solution)/shard_map/ppermute | solution.py:22
  204.2 25.7 %copy-start.31 = (f32[1,3,9,33]{3,0,2,1:T(1,128)S(1)}, f32[1,3,9,33]{3,0,2,1:T(1,128)}, u32[]{:S(2)}) copy-start(f32[1,3,9,33]{3,0,2,1:T(1,128)} %get-tuple-element.557) | copy-start | bytes 10696
  204.2 33.9 %copy-start.30 = (f32[3,9,33]{2,1,0:T(8,128)S(1)}, f32[3,9,33]{2,1,0:T(8,128)}, u32[]{:S(2)}) copy-start(f32[3,9,33]{2,1,0:T(8,128)} %copy.161) | copy-start | bytes 10696
  208.8 10.4 %collective-permute-start.18 = (f32[3,3,1,33]{3,0,2,1:T(4,128)S(1)}, f32[3,3,1,33]{3,0,2,1:T(4,128)S(1)}, u32[]{:S(2)}, u32[]{:S(2)}) collective-permute-start(f32[3,3,1,33]{3,0,2,1:T(4,128)S(1)} %get-tuple-element.656), channel_id=1, source_target_pairs={{0,16},{16,32},{32,48},{48,64},{64,80},{80,96},{96,112},{112,128},... | collective-permute-start | bytes 3572 | tf_op jit(solution)/shard_map/ppermute | solution.py:19
  217.2 8.9 %collective-permute-start.19 = (f32[3,3,1,33]{3,0,2,1:T(4,128)S(1)}, f32[3,3,1,33]{3,0,2,1:T(4,128)S(1)}, u32[]{:S(2)}, u32[]{:S(2)}) collective-permute-start(f32[3,3,1,33]{3,0,2,1:T(4,128)S(1)} %get-tuple-element.657), channel_id=1, source_target_pairs={{16,0},{32,16},{48,32},{64,48},{80,64},{96,80},{112,96},{128,112},... | collective-permute-start | bytes 3572 | tf_op jit(solution)/shard_map/ppermute | solution.py:22
  226.8 4.0 collective-permute-start.20
  228.6 5.7 %collective-permute-start.21 = (f32[3,3,11,1]{3,0,2,1:T(4,128)}, f32[3,3,11,1]{3,0,2,1:T(4,128)S(1)}, u32[]{:S(2)}, u32[]{:S(2)}) collective-permute-start(f32[3,3,11,1]{3,0,2,1:T(4,128)} %get-tuple-element.669), channel_id=1, source_target_pairs={{4,0},{8,4},{12,8},{5,1},{9,5},{13,9},{6,2},{10,6},{14,10},{7,3},{... | collective-permute-start | bytes 1196 | tf_op jit(solution)/shard_map/ppermute | solution.py:22
  234.4 3.6 collective-permute-start.22
  236.7 4.5 collective-permute-start.23
  262.1 6.5 %collective-permute-start.24 = (f32[3,3,1,33]{3,0,2,1:T(4,128)S(1)}, f32[3,3,1,33]{3,0,2,1:T(4,128)S(1)}, u32[]{:S(2)}, u32[]{:S(2)}) collective-permute-start(f32[3,3,1,33]{3,0,2,1:T(4,128)S(1)} %get-tuple-element.649), channel_id=1, source_target_pairs={{0,16},{16,32},{32,48},{48,64},{64,80},{80,96},{96,112},{112,128},... | collective-permute-start | bytes 3572 | tf_op jit(solution)/shard_map/ppermute | solution.py:19
  266.6 8.9 %collective-permute-start.25 = (f32[3,3,1,33]{3,0,2,1:T(4,128)S(1)}, f32[3,3,1,33]{3,0,2,1:T(4,128)S(1)}, u32[]{:S(2)}, u32[]{:S(2)}) collective-permute-start(f32[3,3,1,33]{3,0,2,1:T(4,128)S(1)} %get-tuple-element.650), channel_id=1, source_target_pairs={{16,0},{32,16},{48,32},{64,48},{80,64},{96,80},{112,96},{128,112},... | collective-permute-start | bytes 3572 | tf_op jit(solution)/shard_map/ppermute | solution.py:22
  275.6 4.9 collective-permute-start.26
  279.1 5.0 collective-permute-start.27
  284.3 4.3 collective-permute-start.28
  287.3 4.5 collective-permute-start.29
  311.6 7.6 %collective-permute-start.30 = (f32[3,3,1,33]{3,0,2,1:T(4,128)S(1)}, f32[3,3,1,33]{3,0,2,1:T(4,128)S(1)}, u32[]{:S(2)}, u32[]{:S(2)}) collective-permute-start(f32[3,3,1,33]{3,0,2,1:T(4,128)S(1)} %get-tuple-element.645), channel_id=1, source_target_pairs={{0,16},{16,32},{32,48},{48,64},{64,80},{80,96},{96,112},{112,128},... | collective-permute-start | bytes 3572 | tf_op jit(solution)/shard_map/ppermute | solution.py:19
  317.1 8.9 %collective-permute-start.31 = (f32[3,3,1,33]{3,0,2,1:T(4,128)S(1)}, f32[3,3,1,33]{3,0,2,1:T(4,128)S(1)}, u32[]{:S(2)}, u32[]{:S(2)}) collective-permute-start(f32[3,3,1,33]{3,0,2,1:T(4,128)S(1)} %get-tuple-element.646), channel_id=1, source_target_pairs={{16,0},{32,16},{48,32},{64,48},{80,64},{96,80},{112,96},{128,112},... | collective-permute-start | bytes 3572 | tf_op jit(solution)/shard_map/ppermute | solution.py:22
  326.1 2.8 collective-permute-start.32
  327.6 5.0 collective-permute-start.33
  334.0 6.5 %collective-permute-start.34 = (f32[3,1,11,35]{3,0,2,1:T(4,128)}, f32[3,1,11,35]{3,0,2,1:T(4,128)S(1)}, u32[]{:S(2)}, u32[]{:S(2)}) collective-permute-start(f32[3,1,11,35]{3,0,2,1:T(4,128)} %get-tuple-element.605), channel_id=1, source_target_pairs={{0,1},{1,2},{2,3},{4,5},{5,6},{6,7},{8,9},{9,10},{10,11},{12,13},{... | collective-permute-start | bytes 13868 | tf_op jit(solution)/shard_map/ppermute | solution.py:19
  335.7 4.9 collective-permute-start.35
  363.3 7.2 %collective-permute-start.36 = (f32[3,3,1,33]{3,0,2,1:T(4,128)S(1)}, f32[3,3,1,33]{3,0,2,1:T(4,128)S(1)}, u32[]{:S(2)}, u32[]{:S(2)}) collective-permute-start(f32[3,3,1,33]{3,0,2,1:T(4,128)S(1)} %get-tuple-element.641), channel_id=1, source_target_pairs={{0,16},{16,32},{32,48},{48,64},{64,80},{80,96},{96,112},{112,128},... | collective-permute-start | bytes 3572 | tf_op jit(solution)/shard_map/ppermute | solution.py:19
  368.5 8.9 %collective-permute-start.37 = (f32[3,3,1,33]{3,0,2,1:T(4,128)S(1)}, f32[3,3,1,33]{3,0,2,1:T(4,128)S(1)}, u32[]{:S(2)}, u32[]{:S(2)}) collective-permute-start(f32[3,3,1,33]{3,0,2,1:T(4,128)S(1)} %get-tuple-element.642), channel_id=1, source_target_pairs={{16,0},{32,16},{48,32},{64,48},{80,64},{96,80},{112,96},{128,112},... | collective-permute-start | bytes 3572 | tf_op jit(solution)/shard_map/ppermute | solution.py:22
  377.5 2.7 collective-permute-start.38
  378.9 5.0 collective-permute-start.39
  384.0 4.5 collective-permute-start.40
  387.2 4.5 collective-permute-start.41
  412.3 6.8 %collective-permute-start.42 = (f32[3,3,1,33]{3,0,2,1:T(4,128)S(1)}, f32[3,3,1,33]{3,0,2,1:T(4,128)S(1)}, u32[]{:S(2)}, u32[]{:S(2)}) collective-permute-start(f32[3,3,1,33]{3,0,2,1:T(4,128)S(1)} %get-tuple-element.637), channel_id=1, source_target_pairs={{0,16},{16,32},{32,48},{48,64},{64,80},{80,96},{96,112},{112,128},... | collective-permute-start | bytes 3572 | tf_op jit(solution)/shard_map/ppermute | solution.py:19
  417.1 8.9 %collective-permute-start.43 = (f32[3,3,1,33]{3,0,2,1:T(4,128)S(1)}, f32[3,3,1,33]{3,0,2,1:T(4,128)S(1)}, u32[]{:S(2)}, u32[]{:S(2)}) collective-permute-start(f32[3,3,1,33]{3,0,2,1:T(4,128)S(1)} %get-tuple-element.638), channel_id=1, source_target_pairs={{16,0},{32,16},{48,32},{64,48},{80,64},{96,80},{112,96},{128,112},... | collective-permute-start | bytes 3572 | tf_op jit(solution)/shard_map/ppermute | solution.py:22
  426.0 3.2 collective-permute-start.44
  427.9 5.0 collective-permute-start.45
  433.1 2.7 collective-permute-start.46
  434.5 4.5 collective-permute-start.47
  463.4 6.8 %collective-permute-start.48 = (f32[3,3,1,33]{3,0,2,1:T(4,128)S(1)}, f32[3,3,1,33]{3,0,2,1:T(4,128)S(1)}, u32[]{:S(2)}, u32[]{:S(2)}) collective-permute-start(f32[3,3,1,33]{3,0,2,1:T(4,128)S(1)} %get-tuple-element.633), channel_id=1, source_target_pairs={{0,16},{16,32},{32,48},{48,64},{64,80},{80,96},{96,112},{112,128},... | collective-permute-start | bytes 3572 | tf_op jit(solution)/shard_map/ppermute | solution.py:19
  468.2 8.9 %collective-permute-start.49 = (f32[3,3,1,33]{3,0,2,1:T(4,128)S(1)}, f32[3,3,1,33]{3,0,2,1:T(4,128)S(1)}, u32[]{:S(2)}, u32[]{:S(2)}) collective-permute-start(f32[3,3,1,33]{3,0,2,1:T(4,128)S(1)} %get-tuple-element.634), channel_id=1, source_target_pairs={{16,0},{32,16},{48,32},{64,48},{80,64},{96,80},{112,96},{128,112},... | collective-permute-start | bytes 3572 | tf_op jit(solution)/shard_map/ppermute | solution.py:22
  477.1 3.0 collective-permute-start.50
  478.8 5.0 collective-permute-start.51
  483.9 3.8 collective-permute-start.52
  486.4 4.5 collective-permute-start.53
  (40 other events, 223.2 us)
where the time goes:
time: 519 us; the launch traced here: 511 us
  starting transfers between devices  162 us (31%)
  waiting for transfers between devices  138 us (27%)
  local copies, waits for them, and re-layouts  127 us (24%)
  other arithmetic  74.1 us (14%)
  between operations  10.8 us (2%)
    ppermute x27, waiting for transfers between devices, padded(): lax.ppermute(lax.slice_in_dim(block, 0, width, axis=dim), axis, backward)  109 us
    ppermute x27, starting transfers between devices, padded(): lax.ppermute(lax.slice_in_dim(block, block.shape[dim] - width, None, axis...  104 us
    ppermute x27, starting transfers between devices, padded(): lax.ppermute(lax.slice_in_dim(block, 0, width, axis=dim), axis, backward)  40.8 us
    mul x16, local copies, waits for them, and re-layouts, spread_axis(): upper * weight_shape(weights[1], ndim, axis)  24.5 us
    mul x17, local copies, waits for them, and re-layouts, spread_axis(): lower * weight_shape(weights[0], ndim, axis)  23.2 us
    all_to_all x1, waiting for transfers between devices, shards(): lax.all_to_all(image_slab, 'gx', split_axis=1, concat_axis=0, tiled=True)  19.8 us
    scatter-add x7, local copies, waits for them, and re-layouts, fold_rims(): inner = inner.at[-1].add(moved[-1])  18.9 us
    reshape x7, local copies, waits for them, and re-layouts, collect_axis(): blocks = field.reshape(split_shape)  16.3 us
  transfers between devices with their start and end apart: 56, of which 27 were waited for; matrix products, arithmetic and copies ran while one was open for 6% of the time, Pallas kernels for 0%

commit v1 on v0

--- a/solution.py
+++ b/solution.py
@@ -139,7 +139,12 @@
 
 def shards(image_slab, deformed_slab, shifts):
     image, deformed_block = (
-        lax.all_to_all(image_slab, "gx", split_axis=1, concat_axis=0, tiled=True),
+        jnp.concatenate(
+            lax.all_to_all(
+                jnp.stack(jnp.split(image_slab, lax.axis_size("gx"), axis=1)), "gx", 0, 0
+            ),
+            axis=0,
+        ),
         lax.all_to_all(deformed_slab, "gx", split_axis=1, concat_axis=0, tiled=True),
     )
     z_count, x_count, y_count = image.shape

time: 519 us -> 539 us (1.039)
  local copies, waits for them, and re-layouts: 127 us -> 147 us
    unnamed x106 -> x119, local copies, waits for them, and re-layouts: 14.1 us -> 32.9 us
  transfers between devices with their start and end apart: 56 -> 56, of which waited for: 27 -> 27; matrix products, arithmetic and copies ran while one was open for 6% -> 5% of each run, Pallas kernels for 0% -> 0%
where the time goes in v1:
time: 539 us; the launch traced here: 531 us
  starting transfers between devices  162 us (30%)
  local copies, waits for them, and re-layouts  147 us (27%)
  waiting for transfers between devices  138 us (26%)
  other arithmetic  74.1 us (14%)
  between operations  10.8 us (2%)
    ppermute x27, waiting for transfers between devices, padded(): lax.ppermute(lax.slice_in_dim(block, 0, width, axis=dim), axis, backward)  109 us
    ppermute x27, starting transfers between devices, padded(): lax.ppermute(lax.slice_in_dim(block, block.shape[dim] - width, None, axis...  104 us
    ppermute x27, starting transfers between devices, padded(): lax.ppermute(lax.slice_in_dim(block, 0, width, axis=dim), axis, backward)  40.8 us
    unnamed x119, local copies, waits for them, and re-layouts  32.9 us
    mul x16, local copies, waits for them, and re-layouts, spread_axis(): upper * weight_shape(weights[1], ndim, axis)  24.5 us
    mul x17, local copies, waits for them, and re-layouts, spread_axis(): lower * weight_shape(weights[0], ndim, axis)  23.2 us
    all_to_all x1, waiting for transfers between devices, shards(): lax.all_to_all(jnp.stack(jnp.split(image_slab, lax.axis_size('gx'), axis=...  19.7 us
    scatter-add x7, local copies, waits for them, and re-layouts, fold_rims(): inner = inner.at[-1].add(moved[-1])  18.9 us
  transfers between devices with their start and end apart: 56, of which 27 were waited for; matrix products, arithmetic and copies ran while one was open for 5% of the time, Pallas kernels for 0%

profile of v1, /device:TPU:1, one launch (start us, length us, event | category | flops | bytes accessed | tf_op | source)
XLA Modules:
  0.0 531.4 jit_solution(888674407057983331)
XLA Ops:
  24.3 12.4 %all-to-all-start = ((f32[16,1,64,256]{3,2,1,0:T(8,128)}), f32[16,1,64,256]{3,2,1,0:T(8,128)S(1)}, u32[]{:S(2)}, u32[]{:S(2)}) async-start(f32[16,1,64,256]{3,2,1,0:T(8,128)} %bitcast_dynamic-update-slice_fusion), calls=%async_computation | async-start | bytes 2097152 | tf_op jit(solution)/shard_map/all_to_all | solution.py:143
  38.8 19.7 %all-to-all-done = f32[16,1,64,256]{3,2,1,0:T(8,128)S(1)} async-done(((f32[16,1,64,256]{3,2,1,0:T(8,128)}), f32[16,1,64,256]{3,2,1,0:T(8,128)S(1)}, u32[]{:S(2)}, u32[]{:S(2)}) %all-to-all-start) | async-done | bytes 1048608 | tf_op jit(solution)/shard_map/all_to_all | solution.py:143
  58.5 5.1 all-to-all-start.1
  65.4 7.5 %collective-permute-start = (f32[16,1,256]{2,1,0:T(1,128)S(1)}, f32[16,1,256]{2,1,0:T(1,128)S(1)}, u32[]{:S(2)}, u32[]{:S(2)}) collective-permute-start(f32[16,1,256]{2,1,0:T(1,128)S(1)} %get-tuple-element.579), channel_id=1, source_target_pairs={{0,16},{16,32},{32,48},{48,64},{64,80},{80,96},{96,112},{112,128},... | collective-permute-start | bytes 49160 | tf_op jit(solution)/shard_map/ppermute | solution.py:19
  75.6 11.6 %collective-permute-done.1 = f32[16,1,256]{2,1,0:T(1,128)S(1)} collective-permute-done((f32[16,1,256]{2,1,0:T(1,128)S(1)}, f32[16,1,256]{2,1,0:T(1,128)S(1)}, u32[]{:S(2)}, u32[]{:S(2)}) %collective-permute-start.1) | collective-permute-done | bytes 16416 | tf_op jit(solution)/shard_map/ppermute | solution.py:22
  89.6 10.0 %collective-permute-start.2 = (f32[16,66,1]{1,0,2:T(8,128)S(1)}, f32[16,66,1]{1,0,2:T(8,128)S(1)}, u32[]{:S(2)}, u32[]{:S(2)}) collective-permute-start(f32[16,66,1]{1,0,2:T(8,128)S(1)} %copy.148), channel_id=1, source_target_pairs={{0,4},{4,8},{8,12},{1,5},{5,9},{9,13},{2,6},{6,10},{10,14},{3,7},{... | collective-permute-start | bytes 12680 | tf_op jit(solution)/shard_map/ppermute | solution.py:19
  109.0 4.9 collective-permute-start.5
  113.9 2.3 copy.203
  121.1 2.3 fusion.2
  128.5 3.5 reshape.1874
  132.1 3.3 multiply_reduce_fusion.21
  135.5 3.5 collective-permute-start.6
  141.0 6.9 %collective-permute-done.7 = f32[6,3,1,33]{3,0,2,1:T(8,128)S(1)} collective-permute-done((f32[6,3,1,33]{3,0,2,1:T(8,128)S(1)}, f32[6,3,1,33]{3,0,2,1:T(8,128)S(1)}, u32[]{:S(2)}, u32[]{:S(2)}) %collective-permute-start.7) | collective-permute-done | bytes 2408 | tf_op jit(solution)/shard_map/ppermute | solution.py:22
  148.0 4.4 collective-permute-start.8
  158.3 2.6 collective-permute-start.10
  163.9 2.5 collective-permute-done.11
  170.3 6.3 %collective-permute-start.14 = (f32[16,80,8]{1,2,0:T(8,128)S(1)}, f32[16,80,8]{1,2,0:T(8,128)S(1)}, u32[]{:S(2)}, u32[]{:S(2)}) collective-permute-start(f32[16,80,8]{1,2,0:T(8,128)S(1)} %copy.156), channel_id=1, source_target_pairs={{0,4},{4,8},{8,12},{1,5},{5,9},{9,13},{2,6},{6,10},{10,14},{3,7},{... | collective-permute-start | bytes 122888 | tf_op jit(solution)/shard_map/ppermute | solution.py:19
  180.9 2.9 collective-permute-done.15
  185.7 2.4 pad_maximum_fusion.3
  189.6 3.6 collective-permute-start.16
  199.3 3.5 scatter-add.149
  205.3 8.9 %collective-permute-done.16 = f32[8,80,272]{2,1,0:T(8,128)} collective-permute-done((f32[8,80,272]{2,1,0:T(8,128)}, f32[8,80,272]{2,1,0:T(8,128)}, u32[]{:S(2)}, u32[]{:S(2)}) %collective-permute-start.16) | collective-permute-done | bytes 696352 | tf_op jit(solution)/shard_map/ppermute | solution.py:19
  214.1 4.8 collective-permute-done.17
  218.9 3.6 pad_maximum_fusion
  229.1 8.4 %collective-permute-start.18 = (f32[3,3,1,33]{3,0,2,1:T(4,128)S(1)}, f32[3,3,1,33]{3,0,2,1:T(4,128)S(1)}, u32[]{:S(2)}, u32[]{:S(2)}) collective-permute-start(f32[3,3,1,33]{3,0,2,1:T(4,128)S(1)} %get-tuple-element.656), channel_id=1, source_target_pairs={{0,16},{16,32},{32,48},{48,64},{64,80},{80,96},{96,112},{112,128},... | collective-permute-start | bytes 3572 | tf_op jit(solution)/shard_map/ppermute | solution.py:19
  239.5 6.8 %collective-permute-done.19 = f32[3,3,1,33]{3,0,2,1:T(4,128)S(1)} collective-permute-done((f32[3,3,1,33]{3,0,2,1:T(4,128)S(1)}, f32[3,3,1,33]{3,0,2,1:T(4,128)S(1)}, u32[]{:S(2)}, u32[]{:S(2)}) %collective-permute-start.19) | collective-permute-done | bytes 1220 | tf_op jit(solution)/shard_map/ppermute | solution.py:22
  251.1 3.5 collective-permute-done.21
  258.4 3.2 collective-permute-done.23
  263.3 2.6 scatter-add.159
  272.6 2.7 mul.1701
  282.4 4.4 collective-permute-start.24
  288.9 6.8 %collective-permute-done.25 = f32[3,3,1,33]{3,0,2,1:T(4,128)S(1)} collective-permute-done((f32[3,3,1,33]{3,0,2,1:T(4,128)S(1)}, f32[3,3,1,33]{3,0,2,1:T(4,128)S(1)}, u32[]{:S(2)}, u32[]{:S(2)}) %collective-permute-start.25) | collective-permute-done | bytes 1220 | tf_op jit(solution)/shard_map/ppermute | solution.py:22
  295.8 3.5 collective-permute-start.26
  300.7 3.7 collective-permute-done.27
  304.5 3.0 collective-permute-start.28
  308.9 3.2 collective-permute-done.29
  322.1 2.7 mul.1741
  331.9 5.5 %collective-permute-start.30 = (f32[3,3,1,33]{3,0,2,1:T(4,128)S(1)}, f32[3,3,1,33]{3,0,2,1:T(4,128)S(1)}, u32[]{:S(2)}, u32[]{:S(2)}) collective-permute-start(f32[3,3,1,33]{3,0,2,1:T(4,128)S(1)} %get-tuple-element.645), channel_id=1, source_target_pairs={{0,16},{16,32},{32,48},{48,64},{64,80},{80,96},{96,112},{112,128},... | collective-permute-start | bytes 3572 | tf_op jit(solution)/shard_map/ppermute | solution.py:19
  339.5 6.8 %collective-permute-done.31 = f32[3,3,1,33]{3,0,2,1:T(4,128)S(1)} collective-permute-done((f32[3,3,1,33]{3,0,2,1:T(4,128)S(1)}, f32[3,3,1,33]{3,0,2,1:T(4,128)S(1)}, u32[]{:S(2)}, u32[]{:S(2)}) %collective-permute-start.31) | collective-permute-done | bytes 1220 | tf_op jit(solution)/shard_map/ppermute | solution.py:22
  349.2 3.7 collective-permute-done.33
  383.6 5.2 collective-permute-start.36
  390.9 6.8 %collective-permute-done.37 = f32[3,3,1,33]{3,0,2,1:T(4,128)S(1)} collective-permute-done((f32[3,3,1,33]{3,0,2,1:T(4,128)S(1)}, f32[3,3,1,33]{3,0,2,1:T(4,128)S(1)}, u32[]{:S(2)}, u32[]{:S(2)}) %collective-permute-start.37) | collective-permute-done | bytes 1220 | tf_op jit(solution)/shard_map/ppermute | solution.py:22
  400.5 3.7 collective-permute-done.39
  404.3 3.2 collective-permute-start.40
  408.8 3.2 collective-permute-done.41
  412.9 2.3 scatter-add.189
  417.0 2.7 mul.1810
  421.2 2.7 mul.1813
  427.6 2.7 reshape.1884
  432.6 4.8 collective-permute-start.42
  439.4 6.8 %collective-permute-done.43 = f32[3,3,1,33]{3,0,2,1:T(4,128)S(1)} collective-permute-done((f32[3,3,1,33]{3,0,2,1:T(4,128)S(1)}, f32[3,3,1,33]{3,0,2,1:T(4,128)S(1)}, u32[]{:S(2)}, u32[]{:S(2)}) %collective-permute-start.43) | collective-permute-done | bytes 1220 | tf_op jit(solution)/shard_map/ppermute | solution.py:22
  449.6 3.7 collective-permute-done.45
  456.1 3.2 collective-permute-done.47
  462.2 3.3 scatter-add.199
  468.0 2.7 mul.1846
  472.2 2.7 mul.1849
  478.7 2.7 reshape.1886
  483.6 4.8 collective-permute-start.48
  490.5 6.8 %collective-permute-done.49 = f32[3,3,1,33]{3,0,2,1:T(4,128)S(1)} collective-permute-done((f32[3,3,1,33]{3,0,2,1:T(4,128)S(1)}, f32[3,3,1,33]{3,0,2,1:T(4,128)S(1)}, u32[]{:S(2)}, u32[]{:S(2)}) %collective-permute-start.49) | collective-permute-done | bytes 1220 | tf_op jit(solution)/shard_map/ppermute | solution.py:22
  500.4 3.7 collective-permute-done.51
  504.2 2.5 collective-permute-start.52
  508.0 3.2 collective-permute-done.53
  514.1 2.8 scatter-add.209
  528.4 2.8 bitcast_subtract_fusion
  (498 shorter events, 222.6 us)
Async XLA Ops:
  0.6 36.1 %copy-start.16 = (f32[1,1024,256]{2,1,0:T(8,128)S(1)}, f32[1,1024,256]{2,1,0:T(8,128)}, u32[]{:S(2)}) copy-start(f32[1,1024,256]{2,1,0:T(8,128)} %param.89) | copy-start | bytes 3145732
  24.3 34.2 %all-to-all-start = ((f32[16,1,64,256]{3,2,1,0:T(8,128)}), f32[16,1,64,256]{3,2,1,0:T(8,128)S(1)}, u32[]{:S(2)}, u32[]{:S(2)}) async-start(f32[16,1,64,256]{3,2,1,0:T(8,128)} %bitcast_dynamic-update-slice_fusion), calls=%async_computation | async-start | bytes 2097152 | tf_op jit(solution)/shard_map/all_to_all | solution.py:143
  36.7 38.0 %copy-start.44 = (s32[2,3,1,1,1]{1,4,3,2,0:T(1,128)S(1)}, s32[2,3,1,1,1]{1,4,3,2,0:T(1,128)}, u32[]{:S(2)}) copy-start(s32[2,3,1,1,1]{1,4,3,2,0:T(1,128)} %param.90) | copy-start | bytes 76
  58.5 61.5 %copy-start = (f32[16,1,64,256]{3,2,1,0:T(8,128)}, f32[16,1,64,256]{3,2,1,0:T(8,128)S(1)}, u32[]{:S(2)}) copy-start(f32[16,1,64,256]{3,2,1,0:T(8,128)S(1)} %all-to-all-done) | copy-start | bytes 3145732
  58.5 55.3 %all-to-all-start.1 = ((f32[1,1024,256]{2,0,1:T(1,128)}), f32[1,1024,256]{2,0,1:T(1,128)}, u32[]{:S(2)}, u32[]{:S(2)}) async-start(f32[1,1024,256]{2,0,1:T(1,128)} %copy.155), calls=%async_computation.1 | async-start | bytes 2097152 | tf_op jit(solution)/shard_map/all_to_all | solution.py:148
  65.4 10.2 %collective-permute-start = (f32[16,1,256]{2,1,0:T(1,128)S(1)}, f32[16,1,256]{2,1,0:T(1,128)S(1)}, u32[]{:S(2)}, u32[]{:S(2)}) collective-permute-start(f32[16,1,256]{2,1,0:T(1,128)S(1)} %get-tuple-element.579), channel_id=1, source_target_pairs={{0,16},{16,32},{32,48},{48,64},{64,80},{80,96},{96,112},{112,128},... | collective-permute-start | bytes 49160 | tf_op jit(solution)/shard_map/ppermute | solution.py:19
  72.8 14.3 %collective-permute-start.1 = (f32[16,1,256]{2,1,0:T(1,128)S(1)}, f32[16,1,256]{2,1,0:T(1,128)S(1)}, u32[]{:S(2)}, u32[]{:S(2)}) collective-permute-start(f32[16,1,256]{2,1,0:T(1,128)S(1)} %get-tuple-element.580), channel_id=1, source_target_pairs={{16,0},{32,16},{48,32},{64,48},{80,64},{96,80},{112,96},{128,112},... | collective-permute-start | bytes 49160 | tf_op jit(solution)/shard_map/ppermute | solution.py:22
  89.6 17.2 %collective-permute-start.2 = (f32[16,66,1]{1,0,2:T(8,128)S(1)}, f32[16,66,1]{1,0,2:T(8,128)S(1)}, u32[]{:S(2)}, u32[]{:S(2)}) collective-permute-start(f32[16,66,1]{1,0,2:T(8,128)S(1)} %copy.148), channel_id=1, source_target_pairs={{0,4},{4,8},{8,12},{1,5},{5,9},{9,13},{2,6},{6,10},{10,14},{3,7},{... | collective-permute-start | bytes 12680 | tf_op jit(solution)/shard_map/ppermute | solution.py:19
  99.9 7.3 %collective-permute-start.3 = (f32[16,66,1]{1,0,2:T(8,128)S(1)}, f32[16,66,1]{1,0,2:T(8,128)S(1)}, u32[]{:S(2)}, u32[]{:S(2)}) collective-permute-start(f32[16,66,1]{1,0,2:T(8,128)S(1)} %copy.149), channel_id=1, source_target_pairs={{4,0},{8,4},{12,8},{5,1},{9,5},{13,9},{6,2},{10,6},{14,10},{7,3},{... | collective-permute-start | bytes 12680 | tf_op jit(solution)/shard_map/ppermute | solution.py:22
  107.7 8.5 %collective-permute-start.4 = (f32[1,66,258]{2,1,0:T(8,128)S(1)}, f32[1,66,258]{2,1,0:T(8,128)S(1)}, u32[]{:S(2)}, u32[]{:S(2)}) collective-permute-start(f32[1,66,258]{2,1,0:T(8,128)S(1)} %get-tuple-element.566), channel_id=1, source_target_pairs={{1,0},{2,1},{3,2},{5,4},{6,5},{7,6},{9,8},{10,9},{11,10},{13,12},{... | collective-permute-start | bytes 204344 | tf_op jit(solution)/shard_map/ppermute | solution.py:22
  109.0 7.8 %collective-permute-start.5 = (f32[1,66,258]{2,1,0:T(8,128)S(1)}, f32[1,66,258]{2,1,0:T(8,128)}, u32[]{:S(2)}, u32[]{:S(2)}) collective-permute-start(f32[1,66,258]{2,1,0:T(8,128)S(1)} %get-tuple-element.565), channel_id=1, source_target_pairs={{0,1},{1,2},{2,3},{4,5},{5,6},{6,7},{8,9},{9,10},{10,11},{12,13},{... | collective-permute-start | bytes 204344 | tf_op jit(solution)/shard_map/ppermute | solution.py:19
  132.1 30.1 %copy-start.11 = (f32[3,2,64,256]{3,2,1,0:T(8,128)S(1)}, f32[3,2,64,256]{3,2,1,0:T(8,128)}, u32[]{:S(2)}) copy-start(f32[3,2,64,256]{3,2,1,0:T(8,128)} %get-tuple-element.594) | copy-start | bytes 1179652
  132.1 30.1 %copy-start.46 = (f32[3]{0:T(128)S(1)}, f32[3]{0:T(128)}, u32[]{:S(2)}) copy-start(f32[3]{0:T(128)} %get-tuple-element.689) | copy-start | bytes 40
  135.5 5.6 %collective-permute-start.6 = (f32[6,3,1,33]{3,0,2,1:T(8,128)S(1)}, f32[6,3,1,33]{3,0,2,1:T(8,128)S(1)}, u32[]{:S(2)}, u32[]{:S(2)}) collective-permute-start(f32[6,3,1,33]{3,0,2,1:T(8,128)S(1)} %get-tuple-element.597), channel_id=1, source_target_pairs={{0,16},{16,32},{32,48},{48,64},{64,80},{80,96},{96,112},{112,128},... | collective-permute-start | bytes 7136 | tf_op jit(solution)/shard_map/ppermute | solution.py:19
  139.0 8.9 %collective-permute-start.7 = (f32[6,3,1,33]{3,0,2,1:T(8,128)S(1)}, f32[6,3,1,33]{3,0,2,1:T(8,128)S(1)}, u32[]{:S(2)}, u32[]{:S(2)}) collective-permute-start(f32[6,3,1,33]{3,0,2,1:T(8,128)S(1)} %get-tuple-element.598), channel_id=1, source_target_pairs={{16,0},{32,16},{48,32},{64,48},{80,64},{96,80},{112,96},{128,112},... | collective-permute-start | bytes 7136 | tf_op jit(solution)/shard_map/ppermute | solution.py:22
  148.0 10.1 %collective-permute-start.8 = (f32[6,3,11,1]{3,0,2,1:T(8,128)S(1)}, f32[6,3,11,1]{3,0,2,1:T(8,128)S(1)}, u32[]{:S(2)}, u32[]{:S(2)}) collective-permute-start(f32[6,3,11,1]{3,0,2,1:T(8,128)S(1)} %get-tuple-element.629), channel_id=1, source_target_pairs={{0,4},{4,8},{8,12},{1,5},{5,9},{9,13},{2,6},{6,10},{10,14},{3,7},{... | collective-permute-start | bytes 2384 | tf_op jit(solution)/shard_map/ppermute | solution.py:19
  152.4 5.8 %collective-permute-start.9 = (f32[6,3,11,1]{3,0,2,1:T(8,128)S(1)}, f32[6,3,11,1]{3,0,2,1:T(8,128)S(1)}, u32[]{:S(2)}, u32[]{:S(2)}) collective-permute-start(f32[6,3,11,1]{3,0,2,1:T(8,128)S(1)} %get-tuple-element.630), channel_id=1, source_target_pairs={{4,0},{8,4},{12,8},{5,1},{9,5},{13,9},{6,2},{10,6},{14,10},{7,3},{... | collective-permute-start | bytes 2384 | tf_op jit(solution)/shard_map/ppermute | solution.py:22
  153.8 12.8 %collective-permute-start.12 = (f32[16,8,256]{2,1,0:T(8,128)S(1)}, f32[16,8,256]{2,1,0:T(8,128)S(1)}, u32[]{:S(2)}, u32[]{:S(2)}) collective-permute-start(f32[16,8,256]{2,1,0:T(8,128)S(1)} %get-tuple-element.577), channel_id=1, source_target_pairs={{0,16},{16,32},{32,48},{48,64},{64,80},{80,96},{96,112},{112,128},... | collective-permute-start | bytes 393224 | tf_op jit(solution)/shard_map/ppermute | solution.py:19
  155.9 11.7 %collective-permute-start.13 = (f32[16,8,256]{2,1,0:T(8,128)S(1)}, f32[16,8,256]{2,1,0:T(8,128)S(1)}, u32[]{:S(2)}, u32[]{:S(2)}) collective-permute-start(f32[16,8,256]{2,1,0:T(8,128)S(1)} %get-tuple-element.578), channel_id=1, source_target_pairs={{16,0},{32,16},{48,32},{64,48},{80,64},{96,80},{112,96},{128,112},... | collective-permute-start | bytes 393224 | tf_op jit(solution)/shard_map/ppermute | solution.py:22
  158.3 5.6 %collective-permute-start.10 = (f32[6,1,11,35]{3,0,2,1:T(8,128)S(1)}, f32[6,1,11,35]{3,0,2,1:T(8,128)S(1)}, u32[]{:S(2)}, u32[]{:S(2)}) collective-permute-start(f32[6,1,11,35]{3,0,2,1:T(8,128)S(1)} %get-tuple-element.595), channel_id=1, source_target_pairs={{0,1},{1,2},{2,3},{4,5},{5,6},{6,7},{8,9},{9,10},{10,11},{12,13},{... | collective-permute-start | bytes 27728 | tf_op jit(solution)/shard_map/ppermute | solution.py:19
  160.9 5.5 %collective-permute-start.11 = (f32[6,1,11,35]{3,0,2,1:T(8,128)S(1)}, f32[6,1,11,35]{3,0,2,1:T(8,128)S(1)}, u32[]{:S(2)}, u32[]{:S(2)}) collective-permute-start(f32[6,1,11,35]{3,0,2,1:T(8,128)S(1)} %get-tuple-element.596), channel_id=1, source_target_pairs={{1,0},{2,1},{3,2},{5,4},{6,5},{7,6},{9,8},{10,9},{11,10},{13,12},{... | collective-permute-start | bytes 27728 | tf_op jit(solution)/shard_map/ppermute | solution.py:22
  170.3 9.5 %collective-permute-start.14 = (f32[16,80,8]{1,2,0:T(8,128)S(1)}, f32[16,80,8]{1,2,0:T(8,128)S(1)}, u32[]{:S(2)}, u32[]{:S(2)}) collective-permute-start(f32[16,80,8]{1,2,0:T(8,128)S(1)} %copy.156), channel_id=1, source_target_pairs={{0,4},{4,8},{8,12},{1,5},{5,9},{9,13},{2,6},{6,10},{10,14},{3,7},{... | collective-permute-start | bytes 122888 | tf_op jit(solution)/shard_map/ppermute | solution.py:19
  178.5 5.3 %collective-permute-start.15 = (f32[16,80,8]{1,2,0:T(8,128)}, f32[16,80,8]{1,2,0:T(8,128)}, u32[]{:S(2)}, u32[]{:S(2)}) collective-permute-start(f32[16,80,8]{1,2,0:T(8,128)} %copy.157), channel_id=1, source_target_pairs={{4,0},{8,4},{12,8},{5,1},{9,5},{13,9},{6,2},{10,6},{14,10},{7,3},{... | collective-permute-start | bytes 122888 | tf_op jit(solution)/shard_map/ppermute | solution.py:22
  188.2 30.8 %copy-start.13 = (f32[16,8,256]{2,1,0:T(8,128)S(1)}, f32[16,8,256]{2,1,0:T(8,128)}, u32[]{:S(2)}) copy-start(f32[16,8,256]{2,1,0:T(8,128)} %copy-done.12) | copy-start | bytes 393220
  188.2 30.8 %copy-start.15 = (f32[16,8,256]{2,1,0:T(8,128)S(1)}, f32[16,8,256]{2,1,0:T(8,128)}, u32[]{:S(2)}) copy-start(f32[16,8,256]{2,1,0:T(8,128)} %copy-done.14) | copy-start | bytes 393220
  189.6 24.5 %collective-permute-start.16 = (f32[8,80,272]{2,1,0:T(8,128)}, f32[8,80,272]{2,1,0:T(8,128)}, u32[]{:S(2)}, u32[]{:S(2)}) collective-permute-start(f32[8,80,272]{2,1,0:T(8,128)} %get-tuple-element.570), channel_id=1, source_target_pairs={{0,1},{1,2},{2,3},{4,5},{5,6},{6,7},{8,9},{9,10},{10,11},{12,13},{... | collective-permute-start | bytes 2088968 | tf_op jit(solution)/shard_map/ppermute | solution.py:19
  193.2 25.7 %collective-permute-start.17 = (f32[8,80,272]{2,1,0:T(8,128)}, f32[8,80,272]{2,1,0:T(8,128)}, u32[]{:S(2)}, u32[]{:S(2)}) collective-permute-start(f32[8,80,272]{2,1,0:T(8,128)} %get-tuple-element.571), channel_id=1, source_target_pairs={{1,0},{2,1},{3,2},{5,4},{6,5},{7,6},{9,8},{10,9},{11,10},{13,12},{... | collective-permute-start | bytes 2088968 | tf_op jit(solution)/shard_map/ppermute | solution.py:22
  224.5 33.8 %copy-start.30 = (f32[3,9,33]{2,1,0:T(8,128)S(1)}, f32[3,9,33]{2,1,0:T(8,128)}, u32[]{:S(2)}) copy-start(f32[3,9,33]{2,1,0:T(8,128)} %copy.154) | copy-start | bytes 10696
  229.1 10.4 %collective-permute-start.18 = (f32[3,3,1,33]{3,0,2,1:T(4,128)S(1)}, f32[3,3,1,33]{3,0,2,1:T(4,128)S(1)}, u32[]{:S(2)}, u32[]{:S(2)}) collective-permute-start(f32[3,3,1,33]{3,0,2,1:T(4,128)S(1)} %get-tuple-element.656), channel_id=1, source_target_pairs={{0,16},{16,32},{32,48},{48,64},{64,80},{80,96},{96,112},{112,128},... | collective-permute-start | bytes 3572 | tf_op jit(solution)/shard_map/ppermute | solution.py:19
  237.4 8.9 %collective-permute-start.19 = (f32[3,3,1,33]{3,0,2,1:T(4,128)S(1)}, f32[3,3,1,33]{3,0,2,1:T(4,128)S(1)}, u32[]{:S(2)}, u32[]{:S(2)}) collective-permute-start(f32[3,3,1,33]{3,0,2,1:T(4,128)S(1)} %get-tuple-element.657), channel_id=1, source_target_pairs={{16,0},{32,16},{48,32},{64,48},{80,64},{96,80},{112,96},{128,112},... | collective-permute-start | bytes 3572 | tf_op jit(solution)/shard_map/ppermute | solution.py:22
  247.1 4.0 collective-permute-start.20
  248.9 5.7 %collective-permute-start.21 = (f32[3,3,11,1]{3,0,2,1:T(4,128)}, f32[3,3,11,1]{3,0,2,1:T(4,128)S(1)}, u32[]{:S(2)}, u32[]{:S(2)}) collective-permute-start(f32[3,3,11,1]{3,0,2,1:T(4,128)} %get-tuple-element.669), channel_id=1, source_target_pairs={{4,0},{8,4},{12,8},{5,1},{9,5},{13,9},{6,2},{10,6},{14,10},{7,3},{... | collective-permute-start | bytes 1196 | tf_op jit(solution)/shard_map/ppermute | solution.py:22
  254.7 3.6 collective-permute-start.22
  257.0 4.5 collective-permute-start.23
  282.4 6.5 %collective-permute-start.24 = (f32[3,3,1,33]{3,0,2,1:T(4,128)S(1)}, f32[3,3,1,33]{3,0,2,1:T(4,128)S(1)}, u32[]{:S(2)}, u32[]{:S(2)}) collective-permute-start(f32[3,3,1,33]{3,0,2,1:T(4,128)S(1)} %get-tuple-element.649), channel_id=1, source_target_pairs={{0,16},{16,32},{32,48},{48,64},{64,80},{80,96},{96,112},{112,128},... | collective-permute-start | bytes 3572 | tf_op jit(solution)/shard_map/ppermute | solution.py:19
  286.9 8.9 %collective-permute-start.25 = (f32[3,3,1,33]{3,0,2,1:T(4,128)S(1)}, f32[3,3,1,33]{3,0,2,1:T(4,128)S(1)}, u32[]{:S(2)}, u32[]{:S(2)}) collective-permute-start(f32[3,3,1,33]{3,0,2,1:T(4,128)S(1)} %get-tuple-element.650), channel_id=1, source_target_pairs={{16,0},{32,16},{48,32},{64,48},{80,64},{96,80},{112,96},{128,112},... | collective-permute-start | bytes 3572 | tf_op jit(solution)/shard_map/ppermute | solution.py:22
  295.8 4.9 collective-permute-start.26
  299.4 5.0 collective-permute-start.27
  304.5 4.3 collective-permute-start.28
  307.6 4.5 collective-permute-start.29
  331.9 7.5 %collective-permute-start.30 = (f32[3,3,1,33]{3,0,2,1:T(4,128)S(1)}, f32[3,3,1,33]{3,0,2,1:T(4,128)S(1)}, u32[]{:S(2)}, u32[]{:S(2)}) collective-permute-start(f32[3,3,1,33]{3,0,2,1:T(4,128)S(1)} %get-tuple-element.645), channel_id=1, source_target_pairs={{0,16},{16,32},{32,48},{48,64},{64,80},{80,96},{96,112},{112,128},... | collective-permute-start | bytes 3572 | tf_op jit(solution)/shard_map/ppermute | solution.py:19
  337.4 8.9 %collective-permute-start.31 = (f32[3,3,1,33]{3,0,2,1:T(4,128)S(1)}, f32[3,3,1,33]{3,0,2,1:T(4,128)S(1)}, u32[]{:S(2)}, u32[]{:S(2)}) collective-permute-start(f32[3,3,1,33]{3,0,2,1:T(4,128)S(1)} %get-tuple-element.646), channel_id=1, source_target_pairs={{16,0},{32,16},{48,32},{64,48},{80,64},{96,80},{112,96},{128,112},... | collective-permute-start | bytes 3572 | tf_op jit(solution)/shard_map/ppermute | solution.py:22
  346.4 2.8 collective-permute-start.32
  347.9 5.0 collective-permute-start.33
  354.3 6.5 %collective-permute-start.34 = (f32[3,1,11,35]{3,0,2,1:T(4,128)}, f32[3,1,11,35]{3,0,2,1:T(4,128)S(1)}, u32[]{:S(2)}, u32[]{:S(2)}) collective-permute-start(f32[3,1,11,35]{3,0,2,1:T(4,128)} %get-tuple-element.605), channel_id=1, source_target_pairs={{0,1},{1,2},{2,3},{4,5},{5,6},{6,7},{8,9},{9,10},{10,11},{12,13},{... | collective-permute-start | bytes 13868 | tf_op jit(solution)/shard_map/ppermute | solution.py:19
  355.9 4.9 collective-permute-start.35
  383.6 7.2 %collective-permute-start.36 = (f32[3,3,1,33]{3,0,2,1:T(4,128)S(1)}, f32[3,3,1,33]{3,0,2,1:T(4,128)S(1)}, u32[]{:S(2)}, u32[]{:S(2)}) collective-permute-start(f32[3,3,1,33]{3,0,2,1:T(4,128)S(1)} %get-tuple-element.641), channel_id=1, source_target_pairs={{0,16},{16,32},{32,48},{48,64},{64,80},{80,96},{96,112},{112,128},... | collective-permute-start | bytes 3572 | tf_op jit(solution)/shard_map/ppermute | solution.py:19
  388.8 8.9 %collective-permute-start.37 = (f32[3,3,1,33]{3,0,2,1:T(4,128)S(1)}, f32[3,3,1,33]{3,0,2,1:T(4,128)S(1)}, u32[]{:S(2)}, u32[]{:S(2)}) collective-permute-start(f32[3,3,1,33]{3,0,2,1:T(4,128)S(1)} %get-tuple-element.642), channel_id=1, source_target_pairs={{16,0},{32,16},{48,32},{64,48},{80,64},{96,80},{112,96},{128,112},... | collective-permute-start | bytes 3572 | tf_op jit(solution)/shard_map/ppermute | solution.py:22
  397.8 2.7 collective-permute-start.38
  399.2 5.0 collective-permute-start.39
  404.3 4.5 collective-permute-start.40
  407.5 4.5 collective-permute-start.41
  432.6 6.8 %collective-permute-start.42 = (f32[3,3,1,33]{3,0,2,1:T(4,128)S(1)}, f32[3,3,1,33]{3,0,2,1:T(4,128)S(1)}, u32[]{:S(2)}, u32[]{:S(2)}) collective-permute-start(f32[3,3,1,33]{3,0,2,1:T(4,128)S(1)} %get-tuple-element.637), channel_id=1, source_target_pairs={{0,16},{16,32},{32,48},{48,64},{64,80},{80,96},{96,112},{112,128},... | collective-permute-start | bytes 3572 | tf_op jit(solution)/shard_map/ppermute | solution.py:19
  437.4 8.9 %collective-permute-start.43 = (f32[3,3,1,33]{3,0,2,1:T(4,128)S(1)}, f32[3,3,1,33]{3,0,2,1:T(4,128)S(1)}, u32[]{:S(2)}, u32[]{:S(2)}) collective-permute-start(f32[3,3,1,33]{3,0,2,1:T(4,128)S(1)} %get-tuple-element.638), channel_id=1, source_target_pairs={{16,0},{32,16},{48,32},{64,48},{80,64},{96,80},{112,96},{128,112},... | collective-permute-start | bytes 3572 | tf_op jit(solution)/shard_map/ppermute | solution.py:22
  446.3 3.2 collective-permute-start.44
  448.2 5.0 collective-permute-start.45
  453.4 2.7 collective-permute-start.46
  454.8 4.5 collective-permute-start.47
  483.6 6.8 %collective-permute-start.48 = (f32[3,3,1,33]{3,0,2,1:T(4,128)S(1)}, f32[3,3,1,33]{3,0,2,1:T(4,128)S(1)}, u32[]{:S(2)}, u32[]{:S(2)}) collective-permute-start(f32[3,3,1,33]{3,0,2,1:T(4,128)S(1)} %get-tuple-element.633), channel_id=1, source_target_pairs={{0,16},{16,32},{32,48},{48,64},{64,80},{80,96},{96,112},{112,128},... | collective-permute-start | bytes 3572 | tf_op jit(solution)/shard_map/ppermute | solution.py:19
  488.5 8.9 %collective-permute-start.49 = (f32[3,3,1,33]{3,0,2,1:T(4,128)S(1)}, f32[3,3,1,33]{3,0,2,1:T(4,128)S(1)}, u32[]{:S(2)}, u32[]{:S(2)}) collective-permute-start(f32[3,3,1,33]{3,0,2,1:T(4,128)S(1)} %get-tuple-element.634), channel_id=1, source_target_pairs={{16,0},{32,16},{48,32},{64,48},{80,64},{96,80},{112,96},{128,112},... | collective-permute-start | bytes 3572 | tf_op jit(solution)/shard_map/ppermute | solution.py:22
  497.4 3.0 collective-permute-start.50
  499.1 5.0 collective-permute-start.51
  504.2 3.8 collective-permute-start.52
  506.7 4.5 collective-permute-start.53
  (40 other events, 233.1 us)
